TPU v7x, 512 devices: a whole 4x8x8 slice. The times are simulated.
512 devices in a mesh: section: 4 (over z_hi, core), seq: 32 (over x, y), head: 4 (over z_lo).
Axes of the slice: x: 4, y: 8, z: 8 (z_hi: 2, z_lo: 4; z = z_hi * 4 + z_lo), core: 2. Of those that a mesh axis runs over, the one named last changes fastest.
Arguments:
- query_heads: bfloat16 [4, 6144, 3072], P('section', 'seq', 'head'), may hold values from -6 to 6
- key_heads: bfloat16 [4, 6144, 3072], P('section', 'seq', 'head'), may hold values from -6 to 6
- value_heads: bfloat16 [4, 6144, 3072], P('section', 'seq', 'head'), may hold values from -6 to 6
- stream: bfloat16 [4, 6144, 3072], P('section', 'seq', 'head'), may hold values from -1.5 to 1.5
- out_weight: bfloat16 [4, 3072, 3072], P('section', 'head', 'seq'), may hold values from -0.109375 to 0.109375
- gate_scale: float32 [4, 3072], P('section', 'head'), may hold values from 0.5 to 1.5
- windows: int32 [16, 27], replicated, may hold values from -1 to 15, as said below
Outputs:
- handed: bfloat16 [4, 6144, 3072], P('section', 'seq', 'head')
Inputs may be any that keep to these rules, and one draw needn't show every extreme that they name: `windows`: row t lists, in an order drawn for each row, tile t + dt for every dt in -1, 0, 1 with 0 <= t + dt < 16 and tile t + dt in the same clip as t, and -1 in all its other slots; clips are runs of whole consecutive temporal tiles.
All inputs are finite; a program needn't handle non-finite values.
Results may differ from a plain program's by a relative error of at most 0.012.
Values may be sent and summed in bfloat16 or wider, within the bound.
No kernel may reach another device: no remote copies, remote signals or barrier semaphores. Data moves between devices by JAX's collectives and lax.ppermute only.
A program may use at most 64 MiB of HBM per device.

v0:
```python
from functools import partial
import math
import jax
import jax.numpy as jnp
from jax import lax
from jax.sharding import Mesh, PartitionSpec as P

HD = 128
SPATIAL = 1


def shifted(block, axis, count, distance, wanted):
    devices = range(count)
    route = [(i - distance, i) for i in devices if i - distance in devices and wanted(i)]
    return lax.ppermute(block, axis, route)


def needs(offset):
    if offset == 3:
        return lambda i: i % 2 == 1
    if offset == -3:
        return lambda i: i % 2 == 0
    return lambda i: True


def linear_pairs(sizes, mapping):

    def flat(index):
        value = 0
        for part, size in zip(index, sizes):
            value = value * size + part
        return value

    grid = [[]]
    for size in sizes:
        grid = [index + [part] for index in grid for part in range(size)]
    return [(flat(index), flat(mapping(*index))) for index in grid]


def from_behind(value, axis, steps):
    count = lax.axis_size(axis)
    pairs = [(source, (source + steps) % count) for source in range(count)]
    return lax.ppermute(value, axis, pairs)


def split_heads(slab, head_count):
    return slab.reshape(slab.shape[0], head_count, slab.shape[1] // head_count)


def tile_maxima(key_slab, head_count, spatial_count):
    parts = split_heads(key_slab, head_count).astype(jnp.float32)
    lengths = jnp.sqrt(jnp.sum(parts * parts, axis=2))
    return jnp.max(lengths.reshape(spatial_count, -1, head_count), axis=1)


def slab_keep(nearby, slab_tile, in_range, spatial_count, temporal_count):
    first = jnp.clip(slab_tile, 0, temporal_count - 1) * spatial_count
    return lax.dynamic_slice_in_dim(nearby, first, spatial_count, 1) & in_range


def attend(
    running,
    slab_entry,
    keep,
    query_parts,
    row_bound,
    head_count,
    spatial_count,
    tile_rows,
    score_scale,
):
    weighted, summed = running
    row_count = query_parts.shape[0]
    slab_keys = split_heads(slab_entry[0], head_count)
    slab_values = split_heads(slab_entry[1], head_count)
    scores = (
        jnp.einsum("qhd,khd->hqk", query_parts, slab_keys, preferred_element_type=jnp.float32)
        * score_scale
    )
    row_keep = jnp.broadcast_to(
        keep[:, None, :, None], (spatial_count, tile_rows, spatial_count, tile_rows)
    )
    row_keep = row_keep.reshape(row_count, row_count)
    weights = jnp.where(row_keep[None], jnp.exp(scores - row_bound.T[:, :, None]), 0.0)
    summed = summed + jnp.sum(weights, axis=2)
    weighted = weighted + jnp.einsum(
        "hqk,khd->qhd",
        weights.astype(jnp.bfloat16),
        slab_values,
        preferred_element_type=jnp.float32,
    )
    return (weighted, summed)


def on_device(query_heads, key_heads, value_heads, stream, out_weight, gate_scale, windows):
    queries = query_heads[0]
    own_keys = key_heads[0]
    own_values = value_heads[0]
    row_count, feature_count = queries.shape
    head_count = feature_count // HD
    spatial_count = SPATIAL
    tile_rows = row_count // spatial_count
    tile_count = windows.shape[0]
    temporal_count = tile_count // spatial_count
    score_scale = 1.0 / math.sqrt(HD)
    x_count = lax.axis_size("sx")
    y_count = lax.axis_size("sy")
    head_groups = lax.axis_size("head")
    sections = lax.axis_size("section")
    seq_count = x_count * y_count
    x_index = lax.axis_index("sx")
    y_index = lax.axis_index("sy")
    position = x_index * y_count + y_index
    parity = position % 2
    temporal = position // 2
    allowed = jnp.any(
        windows[:, :, None] == jnp.arange(tile_count, dtype=jnp.int32)[None, None, :], axis=1
    )
    row_allowed = lax.dynamic_index_in_dim(allowed, temporal, 0, keepdims=False)
    seq = ("sx", "sy")
    half = feature_count // 2
    own_heads = head_count // 2
    tile_len = 2 * row_count
    partner = [(i, i ^ 1) for i in range(seq_count)]

    def partner_half(block):
        return lax.dynamic_slice_in_dim(block, (1 - parity) * half, half, 1)

    def own_half(block):
        return lax.dynamic_slice_in_dim(block, parity * half, half, 1)

    sent = lax.ppermute(
        (partner_half(queries), partner_half(own_keys), partner_half(own_values)), seq, partner
    )

    def whole_tile(mine, theirs):
        return jnp.where(
            parity == 0,
            jnp.concatenate([mine, theirs], axis=0),
            jnp.concatenate([theirs, mine], axis=0),
        )

    tile_q = whole_tile(own_half(queries), sent[0])
    tile_k = whole_tile(own_half(own_keys), sent[1])
    tile_v = whole_tile(own_half(own_values), sent[2])
    before = lax.ppermute((tile_k, tile_v), seq, [(i, i + 2) for i in range(seq_count - 2)])
    after = lax.ppermute((tile_k, tile_v), seq, [(i, i - 2) for i in range(2, seq_count)])
    key_tiles = [before, (tile_k, tile_v), after]
    keeps = []
    for step in (-1, 0, 1):
        near = temporal + step
        in_range = (near >= 0) & (near < temporal_count)
        listed = lax.dynamic_index_in_dim(
            row_allowed, jnp.clip(near, 0, temporal_count - 1), 0, keepdims=False
        )
        keeps.append(in_range & listed)
    bound = jnp.zeros((own_heads,), jnp.float32)
    for (keys, _), keep in zip(key_tiles, keeps):
        key_float = keys.reshape(tile_len, own_heads, HD).astype(jnp.float32)
        key_lengths = jnp.sqrt(jnp.sum(key_float * key_float, axis=2))
        bound = jnp.maximum(bound, jnp.where(keep, jnp.max(key_lengths, axis=0), 0.0))
    query_parts = tile_q.reshape(tile_len, own_heads, HD)
    query_float = query_parts.astype(jnp.float32)
    query_lengths = jnp.sqrt(jnp.sum(query_float * query_float, axis=2))
    row_bound = query_lengths * bound[None, :] * score_scale
    weight_block = lax.all_gather(out_weight[0], "sy", axis=1, tiled=True)
    swap = linear_pairs((x_count, head_groups), lambda a, b: (b, a))
    stream_in, gate_in, _ = lax.optimization_barrier((stream[0], gate_scale[0], tile_k))
    stream_block = lax.ppermute(stream_in, ("sx", "head"), swap)
    gate_block = lax.ppermute(gate_in, ("sx", "head"), swap)
    weight_block, row_bound, stream_block, gate_block = lax.optimization_barrier(
        (weight_block, row_bound, stream_block, gate_block)
    )
    weighted = jnp.zeros((tile_len, own_heads, HD), jnp.float32)
    summed = jnp.zeros((own_heads, tile_len), jnp.float32)
    for (keys, values), keep in zip(key_tiles, keeps):
        key_parts = keys.reshape(tile_len, own_heads, HD)
        value_parts = values.reshape(tile_len, own_heads, HD)
        scores = (
            jnp.einsum("qhd,khd->hqk", query_parts, key_parts, preferred_element_type=jnp.float32)
            * score_scale
        )
        weights = jnp.where(keep, jnp.exp(scores - row_bound.T[:, :, None]), 0.0)
        summed = summed + jnp.sum(weights, axis=2)
        weighted = weighted + jnp.einsum(
            "hqk,khd->qhd",
            weights.astype(jnp.bfloat16),
            value_parts,
            preferred_element_type=jnp.float32,
        )
    tile_out = (weighted / summed.T[:, :, None]).astype(jnp.bfloat16).reshape(tile_len, half)
    mine_rows = lax.dynamic_slice_in_dim(tile_out, parity * row_count, row_count, 0)
    their_rows = lax.dynamic_slice_in_dim(tile_out, (1 - parity) * row_count, row_count, 0)
    back = lax.ppermute(their_rows, seq, partner)
    attended = jnp.where(
        parity == 0,
        jnp.concatenate([mine_rows, back], axis=1),
        jnp.concatenate([back, mine_rows], axis=1),
    )
    spread = jnp.broadcast_to(attended[None], (x_count,) + attended.shape)
    token_parts = lax.all_to_all(spread, "sx", 0, 0)
    group_index = lax.axis_index("head")

    def term_for(slab_x):
        part = lax.dynamic_index_in_dim(token_parts, slab_x, 0, keepdims=False)
        return jnp.dot(part, weight_block, preferred_element_type=jnp.float32).astype(jnp.bfloat16)

    received = []
    for shift in range(1, head_groups):
        outgoing = term_for((group_index + shift) % head_groups)
        route = [(g, (g + shift) % head_groups) for g in range(head_groups)]
        received.append(lax.ppermute(outgoing, "head", route))
    mixed = term_for(group_index).astype(jnp.float32)
    for term in received:
        mixed = mixed + term.astype(jnp.float32)
    updated = (stream_block.astype(jnp.float32) + gate_block[None, :] * mixed).astype(jnp.bfloat16)
    hand = linear_pairs(
        (sections, x_count, head_groups), lambda s, a, b: ((s + 1) % sections, b, a)
    )
    handed = lax.ppermute(updated, ("section", "sx", "head"), hand)
    return handed[None]


def solution(mesh):
    sections, seq_count, head_count = mesh.devices.shape
    x_count = 4 if seq_count % 4 == 0 else 1
    split_mesh = Mesh(
        mesh.devices.reshape(sections, x_count, seq_count // x_count, head_count),
        ("section", "sx", "sy", "head"),
    )
    seq = ("sx", "sy")
    in_specs = (
        P("section", seq, "head"),
        P("section", seq, "head"),
        P("section", seq, "head"),
        P("section", seq, "head"),
        P("section", "head", seq),
        P("section", "head"),
        P(),
    )
    out_specs = P("section", seq, "head")
    return jax.shard_map(
        on_device, mesh=split_mesh, in_specs=in_specs, out_specs=out_specs, check_vma=False
    )
```

profile of v0, /device:TPU:153, one launch (start us, length us, event | category | flops | bytes accessed | tf_op | source)
XLA Modules:
  0.0 161.0 jit_solution(1921376385303755416)
XLA Ops:
  6.5 0.7 all-gather.3.cloned.1.call-update
  7.3 1.0 dynamic-slice_bitcast_fusion.2
  8.3 0.0 copy-start.3
  8.3 2.1 %collective-permute-start = (bf16[192,384]{1,0:T(8,128)(2,1)S(1)}, bf16[192,384]{1,0:T(8,128)(2,1)S(1)}, u32[]{:S(2)}, u32[]{:S(2)}) collective-permute-start(bf16[192,384]{1,0:T(8,128)(2,1)S(1)} %get-tuple-element.27), channel_id=1, source_target_pairs={{0,4},{4,0},{8,12},{12,8},{16,20},{20,16},{24,28},{28,24},{32,36},... | collective-permute-start | bytes 442376 | tf_op jit(solution)/shard_map/ppermute | solution.py:132
  10.4 1.0 constant_dynamic-slice_fusion.3
  11.4 3.2 %collective-permute-start.1 = (bf16[192,384]{1,0:T(8,128)(2,1)S(1)}, bf16[192,384]{1,0:T(8,128)(2,1)S(1)}, u32[]{:S(2)}, u32[]{:S(2)}) collective-permute-start(bf16[192,384]{1,0:T(8,128)(2,1)S(1)} %get-tuple-element.26), channel_id=1, source_target_pairs={{0,4},{4,0},{8,12},{12,8},{16,20},{20,16},{24,28},{28,24},{32,36},... | collective-permute-start | bytes 442376 | tf_op jit(solution)/shard_map/ppermute | solution.py:132
  14.7 0.1 constant_dynamic-slice_fusion.2
  14.7 2.1 %collective-permute-start.6 = (bf16[192,384]{1,0:T(8,128)(2,1)S(1)}, bf16[192,384]{1,0:T(8,128)(2,1)S(1)}, u32[]{:S(2)}, u32[]{:S(2)}) collective-permute-start(bf16[192,384]{1,0:T(8,128)(2,1)S(1)} %get-tuple-element.24), channel_id=1, source_target_pairs={{0,4},{4,0},{8,12},{12,8},{16,20},{20,16},{24,28},{28,24},{32,36},... | collective-permute-start | bytes 442376 | tf_op jit(solution)/shard_map/ppermute | solution.py:132
  16.8 0.4 fusion.23
  17.4 0.7 fusion.36
  20.0 0.0 collective-permute-done.1
  20.0 0.8 maximum_select_fusion.4
  20.8 5.4 %collective-permute-start.2 = (bf16[384,384]{1,0:T(8,128)(2,1)}, bf16[384,384]{1,0:T(8,128)(2,1)}, u32[]{:S(2)}, u32[]{:S(2)}) collective-permute-start(bf16[384,384]{1,0:T(8,128)(2,1)} %maximum_select_fusion.4), channel_id=1, source_target_pairs={{0,8},{4,12},{8,16},{12,20},{16,24},{20,28},{24,32},{28,36},{32,40... | collective-permute-start | bytes 884744 | tf_op jit(solution)/shard_map/ppermute | solution.py:146
  26.2 1.9 %collective-permute-start.3 = (bf16[384,384]{1,0:T(8,128)(2,1)}, bf16[384,384]{1,0:T(8,128)(2,1)S(1)}, u32[]{:S(2)}, u32[]{:S(2)}) collective-permute-start(bf16[384,384]{1,0:T(8,128)(2,1)} %maximum_select_fusion.4), channel_id=1, source_target_pairs={{8,0},{12,4},{16,8},{20,12},{24,16},{28,20},{32,24},{36,28},{40,32... | collective-permute-start | bytes 884744 | tf_op jit(solution)/shard_map/ppermute | solution.py:147
  28.2 0.8 maximum_select_fusion.5
  29.0 1.9 %collective-permute-start.8 = (bf16[384,384]{1,0:T(8,128)(2,1)}, bf16[384,384]{1,0:T(8,128)(2,1)S(1)}, u32[]{:S(2)}, u32[]{:S(2)}) collective-permute-start(bf16[384,384]{1,0:T(8,128)(2,1)} %maximum_select_fusion.5), channel_id=1, source_target_pairs={{8,0},{12,4},{16,8},{20,12},{24,16},{28,20},{32,24},{36,28},{40,32... | collective-permute-start | bytes 884744 | tf_op jit(solution)/shard_map/ppermute | solution.py:147
  30.9 5.5 %collective-permute-start.7 = (bf16[384,384]{1,0:T(8,128)(2,1)}, bf16[384,384]{1,0:T(8,128)(2,1)S(1)}, u32[]{:S(2)}, u32[]{:S(2)}) collective-permute-start(bf16[384,384]{1,0:T(8,128)(2,1)} %maximum_select_fusion.5), channel_id=1, source_target_pairs={{0,8},{4,12},{8,16},{12,20},{16,24},{20,28},{24,32},{28,36},{32,40... | collective-permute-start | bytes 884744 | tf_op jit(solution)/shard_map/ppermute | solution.py:146
  36.4 0.5 multiply_reduce_fusion
  37.0 0.1 copy.78
  37.0 0.1 concatenate.71
  37.1 2.8 %collective-permute-start.4 = (bf16[192,768]{1,0:T(8,128)(2,1)}, bf16[192,768]{1,0:T(8,128)(2,1)S(1)}, u32[]{:S(2)}, u32[]{:S(2)}) collective-permute-start(bf16[192,768]{1,0:T(8,128)(2,1)} %bitcast.68), channel_id=1, source_target_pairs={{0,0},{1,32},{2,64},{3,96},{32,1},{33,33},{34,65},{35,97},{64,2},{... | collective-permute-start | bytes 884744 | tf_op jit(solution)/shard_map/ppermute | solution.py:169
  40.0 0.5 multiply_reduce_fusion.1
  40.5 0.4 maximum_select_fusion.2
  41.0 3.3 %collective-permute-done.2 = bf16[384,384]{1,0:T(8,128)(2,1)} collective-permute-done((bf16[384,384]{1,0:T(8,128)(2,1)}, bf16[384,384]{1,0:T(8,128)(2,1)}, u32[]{:S(2)}, u32[]{:S(2)}) %collective-permute-start.2) | collective-permute-done | bytes 294944 | tf_op jit(solution)/shard_map/ppermute | solution.py:146
  44.3 2.4 %collective-permute-start.5 = (f32[768]{0:T(1024)S(1)}, f32[768]{0:T(1024)S(1)}, u32[]{:S(2)}, u32[]{:S(2)}) collective-permute-start(f32[768]{0:T(1024)S(1)} %reduce), channel_id=1, source_target_pairs={{0,0},{1,32},{2,64},{3,96},{32,1},{33,33},{34,65},{35,97},{64,2},{... | collective-permute-start | bytes 9224 | tf_op jit(solution)/shard_map/ppermute | solution.py:170
  46.8 1.2 copy.77
  47.9 0.2 copy.79
  48.2 0.1 multiply_reduce_fusion.3
  48.2 0.1 sqrt_reduce_fusion.2
  48.4 0.1 multiply_reduce_fusion.2
  48.5 0.2 sqrt_reduce_fusion
  48.6 0.1 multiply_multiply_fusion
  48.7 5.0 %collective-permute-done.8 = bf16[384,384]{1,0:T(8,128)(2,1)S(1)} collective-permute-done((bf16[384,384]{1,0:T(8,128)(2,1)}, bf16[384,384]{1,0:T(8,128)(2,1)S(1)}, u32[]{:S(2)}, u32[]{:S(2)}) %collective-permute-start.8) | collective-permute-done | bytes 294944 | tf_op jit(solution)/shard_map/ppermute | solution.py:147
  53.7 0.2 copy.89
  53.9 6.1 %collective-permute-done.7 = bf16[384,384]{1,0:T(8,128)(2,1)S(1)} collective-permute-done((bf16[384,384]{1,0:T(8,128)(2,1)}, bf16[384,384]{1,0:T(8,128)(2,1)S(1)}, u32[]{:S(2)}, u32[]{:S(2)}) %collective-permute-start.7) | collective-permute-done | bytes 294944 | tf_op jit(solution)/shard_map/ppermute | solution.py:146
  60.1 0.2 copy.80
  60.3 7.2 %all-gather.3.cloned.1.call-done = bf16[1,768,768]{1,2,0:T(8,128)(2,1)} async-done(((bf16[1,768,96]{1,2,0:T(8,128)(2,1)}), bf16[1,768,768]{1,2,0:T(8,128)(2,1)}) %all-gather.3.cloned.1.call-update) | async-done | bytes 1179664 | tf_op jit(solution)/shard_map/all_gather | solution.py:166
  67.5 0.1 copy.83
  67.6 0.7 fusion.37
  68.3 0.6 fusion.38
  68.9 0.6 fusion.39
  69.5 0.3 fusion.8
  69.9 0.4 fusion.10
  70.3 0.4 fusion.7
  70.6 0.2 constant_dynamic-slice_fusion.1
  70.8 1.9 %collective-permute-start.9 = (bf16[192,384]{0,1:T(8,128)(2,1)S(1)}, bf16[192,384]{0,1:T(8,128)(2,1)S(1)}, u32[]{:S(2)}, u32[]{:S(2)}) collective-permute-start(bf16[192,384]{0,1:T(8,128)(2,1)S(1)} %get-tuple-element.22), channel_id=1, source_target_pairs={{0,4},{4,0},{8,12},{12,8},{16,20},{20,16},{24,28},{28,24},{32,36},... | collective-permute-start | bytes 442376 | tf_op jit(solution)/shard_map/ppermute | solution.py:194
  72.8 5.2 %collective-permute-done.9 = bf16[192,384]{0,1:T(8,128)(2,1)S(1)} collective-permute-done((bf16[192,384]{0,1:T(8,128)(2,1)S(1)}, bf16[192,384]{0,1:T(8,128)(2,1)S(1)}, u32[]{:S(2)}, u32[]{:S(2)}) %collective-permute-start.9) | collective-permute-done | bytes 147488 | tf_op jit(solution)/shard_map/ppermute | solution.py:194
  78.0 0.1 maximum_select_fusion.3
  78.1 0.2 copy.93
  78.3 1.1 broadcast_in_dim.31
  79.4 3.9 %all-to-all-start = ((bf16[4,192,768]{2,1,0:T(8,128)(2,1)}), bf16[4,192,768]{2,1,0:T(8,128)(2,1)S(1)}, u32[]{:S(2)}, u32[]{:S(2)}) async-start(bf16[4,192,768]{2,1,0:T(8,128)(2,1)} %broadcast_in_dim.31), calls=%async_computation | async-start | bytes 2359296 | tf_op jit(solution)/shard_map/all_to_all | solution.py:201
  83.3 14.5 %all-to-all-done = bf16[4,192,768]{2,1,0:T(8,128)(2,1)S(1)} async-done(((bf16[4,192,768]{2,1,0:T(8,128)(2,1)}), bf16[4,192,768]{2,1,0:T(8,128)(2,1)S(1)}, u32[]{:S(2)}, u32[]{:S(2)}) %all-to-all-start) | async-done | bytes 1179680 | tf_op jit(solution)/shard_map/all_to_all | solution.py:201
  97.8 1.3 convolution_convert_fusion
  99.1 1.9 %collective-permute-start.12 = (bf16[192,768]{1,0:T(8,128)(2,1)}, bf16[192,768]{1,0:T(8,128)(2,1)S(1)}, u32[]{:S(2)}, u32[]{:S(2)}) collective-permute-start(bf16[192,768]{1,0:T(8,128)(2,1)} %convolution_convert_fusion), channel_id=1, source_target_pairs={{0,3},{1,0},{2,1},{3,2},{4,7},{5,4},{6,5},{7,6},{8,11},{9,8},{10,9... | collective-permute-start | bytes 884744 | tf_op jit(solution)/shard_map/ppermute | solution.py:212
  101.0 1.3 convolution_convert_fusion.1
  102.3 6.2 %collective-permute-start.11 = (bf16[192,768]{1,0:T(8,128)(2,1)}, bf16[192,768]{1,0:T(8,128)(2,1)S(1)}, u32[]{:S(2)}, u32[]{:S(2)}) collective-permute-start(bf16[192,768]{1,0:T(8,128)(2,1)} %convolution_convert_fusion.1), channel_id=1, source_target_pairs={{0,2},{1,3},{2,0},{3,1},{4,6},{5,7},{6,4},{7,5},{8,10},{9,11},{10,... | collective-permute-start | bytes 884744 | tf_op jit(solution)/shard_map/ppermute | solution.py:212
  108.4 1.3 convolution_convert_fusion.2
  109.7 1.9 %collective-permute-start.10 = (bf16[192,768]{1,0:T(8,128)(2,1)}, bf16[192,768]{1,0:T(8,128)(2,1)S(1)}, u32[]{:S(2)}, u32[]{:S(2)}) collective-permute-start(bf16[192,768]{1,0:T(8,128)(2,1)} %convolution_convert_fusion.2), channel_id=1, source_target_pairs={{0,1},{1,2},{2,3},{3,0},{4,5},{5,6},{6,7},{7,4},{8,9},{9,10},{10,1... | collective-permute-start | bytes 884744 | tf_op jit(solution)/shard_map/ppermute | solution.py:212
  111.6 13.7 %collective-permute-done.11 = bf16[192,768]{1,0:T(8,128)(2,1)S(1)} collective-permute-done((bf16[192,768]{1,0:T(8,128)(2,1)}, bf16[192,768]{1,0:T(8,128)(2,1)S(1)}, u32[]{:S(2)}, u32[]{:S(2)}) %collective-permute-start.11) | collective-permute-done | bytes 294944 | tf_op jit(solution)/shard_map/ppermute | solution.py:212
  125.3 6.6 %collective-permute-done.10 = bf16[192,768]{1,0:T(8,128)(2,1)S(1)} collective-permute-done((bf16[192,768]{1,0:T(8,128)(2,1)}, bf16[192,768]{1,0:T(8,128)(2,1)S(1)}, u32[]{:S(2)}, u32[]{:S(2)}) %collective-permute-start.10) | collective-permute-done | bytes 294944 | tf_op jit(solution)/shard_map/ppermute | solution.py:212
  131.9 0.6 add_convert_fusion
  132.5 3.1 %collective-permute-start.13 = (bf16[192,768]{1,0:T(8,128)(2,1)S(1)}, bf16[192,768]{1,0:T(8,128)(2,1)S(1)}, u32[]{:S(2)}, u32[]{:S(2)}) collective-permute-start(bf16[192,768]{1,0:T(8,128)(2,1)S(1)} %add_convert_fusion), channel_id=1, source_target_pairs={{0,128},{1,160},{2,192},{3,224},{32,129},{33,161},{34,193},{35,225... | collective-permute-start | bytes 884744 | tf_op jit(solution)/shard_map/ppermute | solution.py:220
  135.5 17.9 %collective-permute-done.13 = bf16[192,768]{1,0:T(8,128)(2,1)S(1)} collective-permute-done((bf16[192,768]{1,0:T(8,128)(2,1)S(1)}, bf16[192,768]{1,0:T(8,128)(2,1)S(1)}, u32[]{:S(2)}, u32[]{:S(2)}) %collective-permute-start.13) | collective-permute-done | bytes 294944 | tf_op jit(solution)/shard_map/ppermute | solution.py:220
  153.5 0.7 copy.118
  (22 shorter events, 0.3 us)
Async XLA Ops:
  6.5 8.1 %copy-start.1 = (bf16[1,192,768]{2,1,0:T(8,128)(2,1)S(1)}, bf16[1,192,768]{2,1,0:T(8,128)(2,1)}, u32[]{:S(2)}) copy-start(bf16[1,192,768]{2,1,0:T(8,128)(2,1)} %param.9) | copy-start | bytes 884740
  6.5 10.3 %copy-start.2 = (s32[16,27]{1,0:T(8,128)S(1)}, s32[16,27]{1,0:T(8,128)}, u32[]{:S(2)}) copy-start(s32[16,27]{1,0:T(8,128)} %param.13) | copy-start | bytes 5188
  6.5 61.0 %all-gather.3.cloned.1.call-start = ((), (), s32[]{:S(2)}) async-start(), calls=%async_computation.1 | async-start | bytes 1327104 | tf_op jit(solution)/shard_map/all_gather | solution.py:166
  8.3 11.6 %copy-start.3 = (f32[1,768]{1,0:T(1,128)S(1)}, f32[1,768]{1,0:T(1,128)}, u32[]{:S(2)}) copy-start(f32[1,768]{1,0:T(1,128)} %param.12) | copy-start | bytes 9220
  8.3 28.8 %collective-permute-start = (bf16[192,384]{1,0:T(8,128)(2,1)S(1)}, bf16[192,384]{1,0:T(8,128)(2,1)S(1)}, u32[]{:S(2)}, u32[]{:S(2)}) collective-permute-start(bf16[192,384]{1,0:T(8,128)(2,1)S(1)} %get-tuple-element.27), channel_id=1, source_target_pairs={{0,4},{4,0},{8,12},{12,8},{16,20},{20,16},{24,28},{28,24},{32,36},... | collective-permute-start | bytes 442376 | tf_op jit(solution)/shard_map/ppermute | solution.py:132
  11.4 8.6 %collective-permute-start.1 = (bf16[192,384]{1,0:T(8,128)(2,1)S(1)}, bf16[192,384]{1,0:T(8,128)(2,1)S(1)}, u32[]{:S(2)}, u32[]{:S(2)}) collective-permute-start(bf16[192,384]{1,0:T(8,128)(2,1)S(1)} %get-tuple-element.26), channel_id=1, source_target_pairs={{0,4},{4,0},{8,12},{12,8},{16,20},{20,16},{24,28},{28,24},{32,36},... | collective-permute-start | bytes 442376 | tf_op jit(solution)/shard_map/ppermute | solution.py:132
  14.7 13.5 %collective-permute-start.6 = (bf16[192,384]{1,0:T(8,128)(2,1)S(1)}, bf16[192,384]{1,0:T(8,128)(2,1)S(1)}, u32[]{:S(2)}, u32[]{:S(2)}) collective-permute-start(bf16[192,384]{1,0:T(8,128)(2,1)S(1)} %get-tuple-element.24), channel_id=1, source_target_pairs={{0,4},{4,0},{8,12},{12,8},{16,20},{20,16},{24,28},{28,24},{32,36},... | collective-permute-start | bytes 442376 | tf_op jit(solution)/shard_map/ppermute | solution.py:132
  20.8 23.5 %collective-permute-start.2 = (bf16[384,384]{1,0:T(8,128)(2,1)}, bf16[384,384]{1,0:T(8,128)(2,1)}, u32[]{:S(2)}, u32[]{:S(2)}) collective-permute-start(bf16[384,384]{1,0:T(8,128)(2,1)} %maximum_select_fusion.4), channel_id=1, source_target_pairs={{0,8},{4,12},{8,16},{12,20},{16,24},{20,28},{24,32},{28,36},{32,40... | collective-permute-start | bytes 884744 | tf_op jit(solution)/shard_map/ppermute | solution.py:146
  26.2 21.7 %collective-permute-start.3 = (bf16[384,384]{1,0:T(8,128)(2,1)}, bf16[384,384]{1,0:T(8,128)(2,1)S(1)}, u32[]{:S(2)}, u32[]{:S(2)}) collective-permute-start(bf16[384,384]{1,0:T(8,128)(2,1)} %maximum_select_fusion.4), channel_id=1, source_target_pairs={{8,0},{12,4},{16,8},{20,12},{24,16},{28,20},{32,24},{36,28},{40,32... | collective-permute-start | bytes 884744 | tf_op jit(solution)/shard_map/ppermute | solution.py:147
  29.0 24.7 %collective-permute-start.8 = (bf16[384,384]{1,0:T(8,128)(2,1)}, bf16[384,384]{1,0:T(8,128)(2,1)S(1)}, u32[]{:S(2)}, u32[]{:S(2)}) collective-permute-start(bf16[384,384]{1,0:T(8,128)(2,1)} %maximum_select_fusion.5), channel_id=1, source_target_pairs={{8,0},{12,4},{16,8},{20,12},{24,16},{28,20},{32,24},{36,28},{40,32... | collective-permute-start | bytes 884744 | tf_op jit(solution)/shard_map/ppermute | solution.py:147
  30.9 29.2 %collective-permute-start.7 = (bf16[384,384]{1,0:T(8,128)(2,1)}, bf16[384,384]{1,0:T(8,128)(2,1)S(1)}, u32[]{:S(2)}, u32[]{:S(2)}) collective-permute-start(bf16[384,384]{1,0:T(8,128)(2,1)} %maximum_select_fusion.5), channel_id=1, source_target_pairs={{0,8},{4,12},{8,16},{12,20},{16,24},{20,28},{24,32},{28,36},{32,40... | collective-permute-start | bytes 884744 | tf_op jit(solution)/shard_map/ppermute | solution.py:146
  37.1 23.2 %collective-permute-start.4 = (bf16[192,768]{1,0:T(8,128)(2,1)}, bf16[192,768]{1,0:T(8,128)(2,1)S(1)}, u32[]{:S(2)}, u32[]{:S(2)}) collective-permute-start(bf16[192,768]{1,0:T(8,128)(2,1)} %bitcast.68), channel_id=1, source_target_pairs={{0,0},{1,32},{2,64},{3,96},{32,1},{33,33},{34,65},{35,97},{64,2},{... | collective-permute-start | bytes 884744 | tf_op jit(solution)/shard_map/ppermute | solution.py:169
  44.3 16.0 %collective-permute-start.5 = (f32[768]{0:T(1024)S(1)}, f32[768]{0:T(1024)S(1)}, u32[]{:S(2)}, u32[]{:S(2)}) collective-permute-start(f32[768]{0:T(1024)S(1)} %reduce), channel_id=1, source_target_pairs={{0,0},{1,32},{2,64},{3,96},{32,1},{33,33},{34,65},{35,97},{64,2},{... | collective-permute-start | bytes 9224 | tf_op jit(solution)/shard_map/ppermute | solution.py:170
  70.8 7.2 %collective-permute-start.9 = (bf16[192,384]{0,1:T(8,128)(2,1)S(1)}, bf16[192,384]{0,1:T(8,128)(2,1)S(1)}, u32[]{:S(2)}, u32[]{:S(2)}) collective-permute-start(bf16[192,384]{0,1:T(8,128)(2,1)S(1)} %get-tuple-element.22), channel_id=1, source_target_pairs={{0,4},{4,0},{8,12},{12,8},{16,20},{20,16},{24,28},{28,24},{32,36},... | collective-permute-start | bytes 442376 | tf_op jit(solution)/shard_map/ppermute | solution.py:194
  79.4 18.4 %copy-start = (bf16[1,768,768]{1,2,0:T(8,128)(2,1)S(1)}, bf16[1,768,768]{1,2,0:T(8,128)(2,1)}, u32[]{:S(2)}) copy-start(bf16[1,768,768]{1,2,0:T(8,128)(2,1)} %all-gather.3.cloned.1.call-done) | copy-start | bytes 3538948
  79.4 18.4 %all-to-all-start = ((bf16[4,192,768]{2,1,0:T(8,128)(2,1)}), bf16[4,192,768]{2,1,0:T(8,128)(2,1)S(1)}, u32[]{:S(2)}, u32[]{:S(2)}) async-start(bf16[4,192,768]{2,1,0:T(8,128)(2,1)} %broadcast_in_dim.31), calls=%async_computation | async-start | bytes 2359296 | tf_op jit(solution)/shard_map/all_to_all | solution.py:201
  99.1 12.5 %collective-permute-start.12 = (bf16[192,768]{1,0:T(8,128)(2,1)}, bf16[192,768]{1,0:T(8,128)(2,1)S(1)}, u32[]{:S(2)}, u32[]{:S(2)}) collective-permute-start(bf16[192,768]{1,0:T(8,128)(2,1)} %convolution_convert_fusion), channel_id=1, source_target_pairs={{0,3},{1,0},{2,1},{3,2},{4,7},{5,4},{6,5},{7,6},{8,11},{9,8},{10,9... | collective-permute-start | bytes 884744 | tf_op jit(solution)/shard_map/ppermute | solution.py:212
  102.3 23.0 %collective-permute-start.11 = (bf16[192,768]{1,0:T(8,128)(2,1)}, bf16[192,768]{1,0:T(8,128)(2,1)S(1)}, u32[]{:S(2)}, u32[]{:S(2)}) collective-permute-start(bf16[192,768]{1,0:T(8,128)(2,1)} %convolution_convert_fusion.1), channel_id=1, source_target_pairs={{0,2},{1,3},{2,0},{3,1},{4,6},{5,7},{6,4},{7,5},{8,10},{9,11},{10,... | collective-permute-start | bytes 884744 | tf_op jit(solution)/shard_map/ppermute | solution.py:212
  109.7 22.2 %collective-permute-start.10 = (bf16[192,768]{1,0:T(8,128)(2,1)}, bf16[192,768]{1,0:T(8,128)(2,1)S(1)}, u32[]{:S(2)}, u32[]{:S(2)}) collective-permute-start(bf16[192,768]{1,0:T(8,128)(2,1)} %convolution_convert_fusion.2), channel_id=1, source_target_pairs={{0,1},{1,2},{2,3},{3,0},{4,5},{5,6},{6,7},{7,4},{8,9},{9,10},{10,1... | collective-permute-start | bytes 884744 | tf_op jit(solution)/shard_map/ppermute | solution.py:212
  132.5 21.0 %collective-permute-start.13 = (bf16[192,768]{1,0:T(8,128)(2,1)S(1)}, bf16[192,768]{1,0:T(8,128)(2,1)S(1)}, u32[]{:S(2)}, u32[]{:S(2)}) collective-permute-start(bf16[192,768]{1,0:T(8,128)(2,1)S(1)} %add_convert_fusion), channel_id=1, source_target_pairs={{0,128},{1,160},{2,192},{3,224},{32,129},{33,161},{34,193},{35,225... | collective-permute-start | bytes 884744 | tf_op jit(solution)/shard_map/ppermute | solution.py:220
Sparse Core Ops, SparseCore 0:
  9.4 58.0 all-gather.2
where the time goes:
time: 162 us; the launch traced here: 161 us
  waiting for transfers between devices  80.3 us (50%)
  starting transfers between devices  46.2 us (29%)
  between operations  15.8 us (10%)
  matrix products  7.39 us (5%)
  local copies, waits for them, and re-layouts  7.23 us (4%)
  other arithmetic  4.11 us (3%)
    ppermute x3, waiting for transfers between devices, on_device(): received.append(lax.ppermute(outgoing, 'head', route))  20.2 us
    ppermute x1, waiting for transfers between devices, on_device(): handed = lax.ppermute(updated, ('section', 'sx', 'head'), hand)  17.9 us
    all_to_all x1, waiting for transfers between devices, on_device(): token_parts = lax.all_to_all(spread, 'sx', 0, 0)  14.5 us
    ppermute x2, starting transfers between devices, on_device(): lax.ppermute((tile_k, tile_v), seq, [(i, i + 2) for i in range(seq_count...  10.9 us
    ppermute x3, starting transfers between devices, on_device(): received.append(lax.ppermute(outgoing, 'head', route))  9.97 us
    ppermute x2, waiting for transfers between devices, on_device(): lax.ppermute((tile_k, tile_v), seq, [(i, i + 2) for i in range(seq_count...  9.49 us
    ppermute x3, starting transfers between devices, on_device(): lax.ppermute((partner_half(queries), partner_half(own_keys), partner_half...  7.35 us
    all_gather x1, waiting for transfers between devices, on_device(): weight_block = lax.all_gather(out_weight[0], 'sy', axis=1, tiled=True)  7.23 us
  transfers between devices with their start and end apart: 16, of which 9 were waited for; matrix products, arithmetic and copies ran while one was open for 7% of the time, Pallas kernels for 0%

commit v1 on v0

--- a/solution.py
+++ b/solution.py
@@ -7,6 +7,13 @@
 
 HD = 128
 SPATIAL = 1
+
+
+def deliver_runs(local_x):
+    x_new = jax.lax.psum(1, "sy")
+    mid_arr = jnp.stack([local_x] * x_new, 0)
+    s_next = jax.lax.all_to_all(mid_arr, axis_name="sy", split_axis=0, concat_axis=0)
+    return jnp.concatenate(s_next, 1)
 
 
 def shifted(block, axis, count, distance, wanted):
@@ -163,7 +170,7 @@
     query_float = query_parts.astype(jnp.float32)
     query_lengths = jnp.sqrt(jnp.sum(query_float * query_float, axis=2))
     row_bound = query_lengths * bound[None, :] * score_scale
-    weight_block = lax.all_gather(out_weight[0], "sy", axis=1, tiled=True)
+    weight_block = deliver_runs(out_weight[0])
     swap = linear_pairs((x_count, head_groups), lambda a, b: (b, a))
     stream_in, gate_in, _ = lax.optimization_barrier((stream[0], gate_scale[0], tile_k))
     stream_block = lax.ppermute(stream_in, ("sx", "head"), swap)

time: 162 us -> 174 us (1.074)
  the two profiles are of different devices: /device:TPU:153 before, /device:TPU:60 now
where the time goes in v1:
time: 174 us; the launch traced here: 173 us
  starting transfers between devices  75.5 us (43%)
  waiting for transfers between devices  72.2 us (41%)
  local copies, waits for them, and re-layouts  11.3 us (6%)
  matrix products  7.65 us (4%)
  other arithmetic  4.1 us (2%)
  between operations  2.36 us (1%)
    ppermute x3, waiting for transfers between devices, on_device(): lax.ppermute((partner_half(queries), partner_half(own_keys), partner_half...  21.7 us
    ppermute x3, starting transfers between devices, on_device(): received.append(lax.ppermute(outgoing, 'head', route))  19.3 us
    ppermute x1, waiting for transfers between devices, on_device(): handed = lax.ppermute(updated, ('section', 'sx', 'head'), hand)  15.9 us
    ppermute x3, waiting for transfers between devices, on_device(): received.append(lax.ppermute(outgoing, 'head', route))  14.6 us
    all_to_all x1, waiting for transfers between devices, on_device(): token_parts = lax.all_to_all(spread, 'sx', 0, 0)  10.9 us
    ppermute x3, starting transfers between devices, on_device(): lax.ppermute((partner_half(queries), partner_half(own_keys), partner_half...  9.34 us
    ppermute x2, starting transfers between devices, on_device(): lax.ppermute((tile_k, tile_v), seq, [(i, i - 2) for i in range(2, seq_cou...  8.3 us
    ppermute x2, starting transfers between devices, on_device(): lax.ppermute((tile_k, tile_v), seq, [(i, i + 2) for i in range(seq_count...  7.28 us
  transfers between devices with their start and end apart: 16, of which 8 were waited for; matrix products, arithmetic and copies ran while one was open for 8% of the time, Pallas kernels for 0%

profile of v1, /device:TPU:60, one launch (start us, length us, event | category | flops | bytes accessed | tf_op | source)
XLA Modules:
  0.0 173.1 jit_solution(15884435818713380871)
XLA Ops:
  0.0 2.0 %stack.3 = bf16[8,768,96]{1,2,0:T(8,128)(2,1)} broadcast(bf16[768,96]{0,1:T(8,128)(2,1)} %bitcast.71), dimensions={1,2} | broadcast | bytes 1327104 | tf_op jit(solution)/shard_map/stack | solution.py:14
  2.0 7.0 %all-to-all-start = ((bf16[8,768,96]{1,2,0:T(8,128)(2,1)}), bf16[8,768,96]{1,2,0:T(8,128)(2,1)S(1)}, u32[]{:S(2)}, u32[]{:S(2)}) async-start(bf16[8,768,96]{1,2,0:T(8,128)(2,1)} %stack.3), calls=%async_computation | async-start | bytes 2359296 | tf_op jit(solution)/shard_map/all_to_all | solution.py:15
  9.1 0.0 copy-start.5
  9.1 3.5 %collective-permute-start = (bf16[192,384]{1,0:T(8,128)(2,1)S(1)}, bf16[192,384]{1,0:T(8,128)(2,1)S(1)}, u32[]{:S(2)}, u32[]{:S(2)}) collective-permute-start(bf16[192,384]{1,0:T(8,128)(2,1)S(1)} %get-tuple-element.27), channel_id=1, source_target_pairs={{0,4},{4,0},{8,12},{12,8},{16,20},{20,16},{24,28},{28,24},{32,36},... | collective-permute-start | bytes 442376 | tf_op jit(solution)/shard_map/ppermute | solution.py:139
  12.6 0.1 constant_dynamic-slice_fusion.3
  12.7 2.5 %collective-permute-start.1 = (bf16[192,384]{1,0:T(8,128)(2,1)S(1)}, bf16[192,384]{1,0:T(8,128)(2,1)S(1)}, u32[]{:S(2)}, u32[]{:S(2)}) collective-permute-start(bf16[192,384]{1,0:T(8,128)(2,1)S(1)} %get-tuple-element.26), channel_id=1, source_target_pairs={{0,4},{4,0},{8,12},{12,8},{16,20},{20,16},{24,28},{28,24},{32,36},... | collective-permute-start | bytes 442376 | tf_op jit(solution)/shard_map/ppermute | solution.py:139
  15.1 0.1 constant_dynamic-slice_fusion.2
  15.2 3.4 %collective-permute-start.6 = (bf16[192,384]{1,0:T(8,128)(2,1)S(1)}, bf16[192,384]{1,0:T(8,128)(2,1)S(1)}, u32[]{:S(2)}, u32[]{:S(2)}) collective-permute-start(bf16[192,384]{1,0:T(8,128)(2,1)S(1)} %get-tuple-element.24), channel_id=1, source_target_pairs={{0,4},{4,0},{8,12},{12,8},{16,20},{20,16},{24,28},{28,24},{32,36},... | collective-permute-start | bytes 442376 | tf_op jit(solution)/shard_map/ppermute | solution.py:139
  18.6 0.4 fusion.23
  19.2 0.7 fusion.36
  21.8 21.7 %collective-permute-done.1 = bf16[192,384]{1,0:T(8,128)(2,1)S(1)} collective-permute-done((bf16[192,384]{1,0:T(8,128)(2,1)S(1)}, bf16[192,384]{1,0:T(8,128)(2,1)S(1)}, u32[]{:S(2)}, u32[]{:S(2)}) %collective-permute-start.1) | collective-permute-done | bytes 147488 | tf_op jit(solution)/shard_map/ppermute | solution.py:139
  43.5 0.8 maximum_select_fusion.4
  44.3 2.9 %collective-permute-start.2 = (bf16[384,384]{1,0:T(8,128)(2,1)}, bf16[384,384]{1,0:T(8,128)(2,1)}, u32[]{:S(2)}, u32[]{:S(2)}) collective-permute-start(bf16[384,384]{1,0:T(8,128)(2,1)} %maximum_select_fusion.4), channel_id=1, source_target_pairs={{0,8},{4,12},{8,16},{12,20},{16,24},{20,28},{24,32},{28,36},{32,40... | collective-permute-start | bytes 884744 | tf_op jit(solution)/shard_map/ppermute | solution.py:153
  47.2 3.8 %collective-permute-start.3 = (bf16[384,384]{1,0:T(8,128)(2,1)}, bf16[384,384]{1,0:T(8,128)(2,1)}, u32[]{:S(2)}, u32[]{:S(2)}) collective-permute-start(bf16[384,384]{1,0:T(8,128)(2,1)} %maximum_select_fusion.4), channel_id=1, source_target_pairs={{8,0},{12,4},{16,8},{20,12},{24,16},{28,20},{32,24},{36,28},{40,32... | collective-permute-start | bytes 884744 | tf_op jit(solution)/shard_map/ppermute | solution.py:154
  51.0 0.8 maximum_select_fusion.5
  51.8 4.5 %collective-permute-start.8 = (bf16[384,384]{1,0:T(8,128)(2,1)}, bf16[384,384]{1,0:T(8,128)(2,1)}, u32[]{:S(2)}, u32[]{:S(2)}) collective-permute-start(bf16[384,384]{1,0:T(8,128)(2,1)} %maximum_select_fusion.5), channel_id=1, source_target_pairs={{8,0},{12,4},{16,8},{20,12},{24,16},{28,20},{32,24},{36,28},{40,32... | collective-permute-start | bytes 884744 | tf_op jit(solution)/shard_map/ppermute | solution.py:154
  56.4 4.3 %collective-permute-start.7 = (bf16[384,384]{1,0:T(8,128)(2,1)}, bf16[384,384]{1,0:T(8,128)(2,1)}, u32[]{:S(2)}, u32[]{:S(2)}) collective-permute-start(bf16[384,384]{1,0:T(8,128)(2,1)} %maximum_select_fusion.5), channel_id=1, source_target_pairs={{0,8},{4,12},{8,16},{12,20},{16,24},{20,28},{24,32},{28,36},{32,40... | collective-permute-start | bytes 884744 | tf_op jit(solution)/shard_map/ppermute | solution.py:153
  60.7 0.5 multiply_reduce_fusion
  61.3 0.1 copy.79
  61.4 0.1 concatenate.71
  61.5 6.0 %collective-permute-start.4 = (bf16[192,768]{1,0:T(8,128)(2,1)}, bf16[192,768]{1,0:T(8,128)(2,1)}, u32[]{:S(2)}, u32[]{:S(2)}) collective-permute-start(bf16[192,768]{1,0:T(8,128)(2,1)} %bitcast.72), channel_id=1, source_target_pairs={{0,0},{1,32},{2,64},{3,96},{32,1},{33,33},{34,65},{35,97},{64,2},{... | collective-permute-start | bytes 884744 | tf_op jit(solution)/shard_map/ppermute | solution.py:176
  67.5 0.5 multiply_reduce_fusion.1
  68.1 0.4 maximum_select_fusion.2
  68.5 3.1 %collective-permute-start.5 = (f32[768]{0:T(1024)S(1)}, f32[768]{0:T(1024)S(1)}, u32[]{:S(2)}, u32[]{:S(2)}) collective-permute-start(f32[768]{0:T(1024)S(1)} %reduce), channel_id=1, source_target_pairs={{0,0},{1,32},{2,64},{3,96},{32,1},{33,33},{34,65},{35,97},{64,2},{... | collective-permute-start | bytes 9224 | tf_op jit(solution)/shard_map/ppermute | solution.py:177
  71.7 1.2 copy.78
  72.8 0.3 collective-permute-done.3
  73.2 1.2 copy.80
  74.3 0.1 multiply_reduce_fusion.3
  74.4 0.1 sqrt_reduce_fusion.2
  74.5 0.1 multiply_reduce_fusion.2
  74.6 0.2 sqrt_reduce_fusion
  74.8 0.1 multiply_multiply_fusion
  74.9 3.1 %collective-permute-done.8 = bf16[384,384]{1,0:T(8,128)(2,1)} collective-permute-done((bf16[384,384]{1,0:T(8,128)(2,1)}, bf16[384,384]{1,0:T(8,128)(2,1)}, u32[]{:S(2)}, u32[]{:S(2)}) %collective-permute-start.8) | collective-permute-done | bytes 294944 | tf_op jit(solution)/shard_map/ppermute | solution.py:154
  78.0 1.2 copy.90
  79.2 1.8 %copy.81 = bf16[384,384]{0,1:T(8,128)(2,1)} copy(bf16[384,384]{1,0:T(8,128)(2,1)} %collective-permute-done.7) | data formatting | bytes 589824 | tf_op jit(solution)/shard_map/ppermute | solution.py:153
  81.0 0.1 copy.84
  81.1 0.7 fusion.37
  81.8 0.6 fusion.38
  82.4 0.6 fusion.39
  83.0 0.3 fusion.8
  83.4 0.0 copy-start.3
  83.4 0.4 fusion.10
  83.8 0.5 copy-done.3
  84.3 0.3 fusion.7
  84.7 0.2 constant_dynamic-slice_fusion.1
  84.9 1.9 %collective-permute-start.9 = (bf16[192,384]{0,1:T(8,128)(2,1)S(1)}, bf16[192,384]{0,1:T(8,128)(2,1)S(1)}, u32[]{:S(2)}, u32[]{:S(2)}) collective-permute-start(bf16[192,384]{0,1:T(8,128)(2,1)S(1)} %get-tuple-element.22), channel_id=1, source_target_pairs={{0,4},{4,0},{8,12},{12,8},{16,20},{20,16},{24,28},{28,24},{32,36},... | collective-permute-start | bytes 442376 | tf_op jit(solution)/shard_map/ppermute | solution.py:201
  86.8 5.6 %collective-permute-done.9 = bf16[192,384]{0,1:T(8,128)(2,1)S(1)} collective-permute-done((bf16[192,384]{0,1:T(8,128)(2,1)S(1)}, bf16[192,384]{0,1:T(8,128)(2,1)S(1)}, u32[]{:S(2)}, u32[]{:S(2)}) %collective-permute-start.9) | collective-permute-done | bytes 147488 | tf_op jit(solution)/shard_map/ppermute | solution.py:201
  92.4 0.1 maximum_select_fusion.3
  92.6 0.2 copy.94
  92.7 1.1 broadcast_in_dim.31
  93.8 6.1 %all-to-all-start.1 = ((bf16[4,192,768]{2,1,0:T(8,128)(2,1)}), bf16[4,192,768]{2,1,0:T(8,128)(2,1)S(1)}, u32[]{:S(2)}, u32[]{:S(2)}) async-start(bf16[4,192,768]{2,1,0:T(8,128)(2,1)} %broadcast_in_dim.31), calls=%async_computation.1 | async-start | bytes 2359296 | tf_op jit(solution)/shard_map/all_to_all | solution.py:208
  100.0 10.9 %all-to-all-done.1 = bf16[4,192,768]{2,1,0:T(8,128)(2,1)S(1)} async-done(((bf16[4,192,768]{2,1,0:T(8,128)(2,1)}), bf16[4,192,768]{2,1,0:T(8,128)(2,1)S(1)}, u32[]{:S(2)}, u32[]{:S(2)}) %all-to-all-start.1) | async-done | bytes 1179680 | tf_op jit(solution)/shard_map/all_to_all | solution.py:208
  110.8 0.6 convolution_convert_fusion
  111.4 15.0 %collective-permute-start.12 = (bf16[192,768]{1,0:T(8,128)(2,1)S(1)}, bf16[192,768]{1,0:T(8,128)(2,1)S(1)}, u32[]{:S(2)}, u32[]{:S(2)}) collective-permute-start(bf16[192,768]{1,0:T(8,128)(2,1)S(1)} %convolution_convert_fusion), channel_id=1, source_target_pairs={{0,3},{1,0},{2,1},{3,2},{4,7},{5,4},{6,5},{7,6},{8,11},{9,8},{10,9... | collective-permute-start | bytes 884744 | tf_op jit(solution)/shard_map/ppermute | solution.py:219
  126.4 1.3 convolution_convert_fusion.1
  127.6 1.9 %collective-permute-start.11 = (bf16[192,768]{1,0:T(8,128)(2,1)}, bf16[192,768]{1,0:T(8,128)(2,1)S(1)}, u32[]{:S(2)}, u32[]{:S(2)}) collective-permute-start(bf16[192,768]{1,0:T(8,128)(2,1)} %convolution_convert_fusion.1), channel_id=1, source_target_pairs={{0,2},{1,3},{2,0},{3,1},{4,6},{5,7},{6,4},{7,5},{8,10},{9,11},{10,... | collective-permute-start | bytes 884744 | tf_op jit(solution)/shard_map/ppermute | solution.py:219
  129.5 1.3 convolution_convert_fusion.2
  130.8 2.5 %collective-permute-start.10 = (bf16[192,768]{1,0:T(8,128)(2,1)}, bf16[192,768]{1,0:T(8,128)(2,1)S(1)}, u32[]{:S(2)}, u32[]{:S(2)}) collective-permute-start(bf16[192,768]{1,0:T(8,128)(2,1)} %convolution_convert_fusion.2), channel_id=1, source_target_pairs={{0,1},{1,2},{2,3},{3,0},{4,5},{5,6},{6,7},{7,4},{8,9},{9,10},{10,1... | collective-permute-start | bytes 884744 | tf_op jit(solution)/shard_map/ppermute | solution.py:219
  133.3 0.5 collective-permute-done.12
  133.8 14.1 %collective-permute-done.11 = bf16[192,768]{1,0:T(8,128)(2,1)S(1)} collective-permute-done((bf16[192,768]{1,0:T(8,128)(2,1)}, bf16[192,768]{1,0:T(8,128)(2,1)S(1)}, u32[]{:S(2)}, u32[]{:S(2)}) %collective-permute-start.11) | collective-permute-done | bytes 294944 | tf_op jit(solution)/shard_map/ppermute | solution.py:219
  147.9 1.6 add_convert_fusion
  149.5 7.0 %collective-permute-start.13 = (bf16[192,768]{1,0:T(8,128)(2,1)S(1)}, bf16[192,768]{1,0:T(8,128)(2,1)S(1)}, u32[]{:S(2)}, u32[]{:S(2)}) collective-permute-start(bf16[192,768]{1,0:T(8,128)(2,1)S(1)} %add_convert_fusion), channel_id=1, source_target_pairs={{0,128},{1,160},{2,192},{3,224},{32,129},{33,161},{34,193},{35,225... | collective-permute-start | bytes 884744 | tf_op jit(solution)/shard_map/ppermute | solution.py:227
  156.5 15.9 %collective-permute-done.13 = bf16[192,768]{1,0:T(8,128)(2,1)S(1)} collective-permute-done((bf16[192,768]{1,0:T(8,128)(2,1)S(1)}, bf16[192,768]{1,0:T(8,128)(2,1)S(1)}, u32[]{:S(2)}, u32[]{:S(2)}) %collective-permute-start.13) | collective-permute-done | bytes 294944 | tf_op jit(solution)/shard_map/ppermute | solution.py:227
  172.4 0.7 copy.119
  (26 shorter events, 0.3 us)
Async XLA Ops:
  2.0 7.0 %copy-start = (bf16[1,192,768]{2,1,0:T(8,128)(2,1)S(1)}, bf16[1,192,768]{2,1,0:T(8,128)(2,1)}, u32[]{:S(2)}) copy-start(bf16[1,192,768]{2,1,0:T(8,128)(2,1)} %param.7) | copy-start | bytes 884740
  2.0 10.6 %copy-start.1 = (bf16[1,192,768]{2,1,0:T(8,128)(2,1)S(1)}, bf16[1,192,768]{2,1,0:T(8,128)(2,1)}, u32[]{:S(2)}) copy-start(bf16[1,192,768]{2,1,0:T(8,128)(2,1)} %param.8) | copy-start | bytes 884740
  2.0 79.0 %all-to-all-start = ((bf16[8,768,96]{1,2,0:T(8,128)(2,1)}), bf16[8,768,96]{1,2,0:T(8,128)(2,1)S(1)}, u32[]{:S(2)}, u32[]{:S(2)}) async-start(bf16[8,768,96]{1,2,0:T(8,128)(2,1)} %stack.3), calls=%async_computation | async-start | bytes 2359296 | tf_op jit(solution)/shard_map/all_to_all | solution.py:15
  9.0 6.1 %copy-start.2 = (bf16[1,192,768]{2,1,0:T(8,128)(2,1)S(1)}, bf16[1,192,768]{2,1,0:T(8,128)(2,1)}, u32[]{:S(2)}) copy-start(bf16[1,192,768]{2,1,0:T(8,128)(2,1)} %param.9) | copy-start | bytes 884740
  9.0 9.6 %copy-start.4 = (s32[16,27]{1,0:T(8,128)S(1)}, s32[16,27]{1,0:T(8,128)}, u32[]{:S(2)}) copy-start(s32[16,27]{1,0:T(8,128)} %param.13) | copy-start | bytes 5188
  9.1 12.7 %copy-start.5 = (f32[1,768]{1,0:T(1,128)S(1)}, f32[1,768]{1,0:T(1,128)}, u32[]{:S(2)}) copy-start(f32[1,768]{1,0:T(1,128)} %param.12) | copy-start | bytes 9220
  9.1 52.4 %collective-permute-start = (bf16[192,384]{1,0:T(8,128)(2,1)S(1)}, bf16[192,384]{1,0:T(8,128)(2,1)S(1)}, u32[]{:S(2)}, u32[]{:S(2)}) collective-permute-start(bf16[192,384]{1,0:T(8,128)(2,1)S(1)} %get-tuple-element.27), channel_id=1, source_target_pairs={{0,4},{4,0},{8,12},{12,8},{16,20},{20,16},{24,28},{28,24},{32,36},... | collective-permute-start | bytes 442376 | tf_op jit(solution)/shard_map/ppermute | solution.py:139
  12.7 30.8 %collective-permute-start.1 = (bf16[192,384]{1,0:T(8,128)(2,1)S(1)}, bf16[192,384]{1,0:T(8,128)(2,1)S(1)}, u32[]{:S(2)}, u32[]{:S(2)}) collective-permute-start(bf16[192,384]{1,0:T(8,128)(2,1)S(1)} %get-tuple-element.26), channel_id=1, source_target_pairs={{0,4},{4,0},{8,12},{12,8},{16,20},{20,16},{24,28},{28,24},{32,36},... | collective-permute-start | bytes 442376 | tf_op jit(solution)/shard_map/ppermute | solution.py:139
  15.2 35.9 %collective-permute-start.6 = (bf16[192,384]{1,0:T(8,128)(2,1)S(1)}, bf16[192,384]{1,0:T(8,128)(2,1)S(1)}, u32[]{:S(2)}, u32[]{:S(2)}) collective-permute-start(bf16[192,384]{1,0:T(8,128)(2,1)S(1)} %get-tuple-element.24), channel_id=1, source_target_pairs={{0,4},{4,0},{8,12},{12,8},{16,20},{20,16},{24,28},{28,24},{32,36},... | collective-permute-start | bytes 442376 | tf_op jit(solution)/shard_map/ppermute | solution.py:139
  44.3 24.2 %collective-permute-start.2 = (bf16[384,384]{1,0:T(8,128)(2,1)}, bf16[384,384]{1,0:T(8,128)(2,1)}, u32[]{:S(2)}, u32[]{:S(2)}) collective-permute-start(bf16[384,384]{1,0:T(8,128)(2,1)} %maximum_select_fusion.4), channel_id=1, source_target_pairs={{0,8},{4,12},{8,16},{12,20},{16,24},{20,28},{24,32},{28,36},{32,40... | collective-permute-start | bytes 884744 | tf_op jit(solution)/shard_map/ppermute | solution.py:153
  47.2 25.9 %collective-permute-start.3 = (bf16[384,384]{1,0:T(8,128)(2,1)}, bf16[384,384]{1,0:T(8,128)(2,1)}, u32[]{:S(2)}, u32[]{:S(2)}) collective-permute-start(bf16[384,384]{1,0:T(8,128)(2,1)} %maximum_select_fusion.4), channel_id=1, source_target_pairs={{8,0},{12,4},{16,8},{20,12},{24,16},{28,20},{32,24},{36,28},{40,32... | collective-permute-start | bytes 884744 | tf_op jit(solution)/shard_map/ppermute | solution.py:154
  51.8 26.2 %collective-permute-start.8 = (bf16[384,384]{1,0:T(8,128)(2,1)}, bf16[384,384]{1,0:T(8,128)(2,1)}, u32[]{:S(2)}, u32[]{:S(2)}) collective-permute-start(bf16[384,384]{1,0:T(8,128)(2,1)} %maximum_select_fusion.5), channel_id=1, source_target_pairs={{8,0},{12,4},{16,8},{20,12},{24,16},{28,20},{32,24},{36,28},{40,32... | collective-permute-start | bytes 884744 | tf_op jit(solution)/shard_map/ppermute | solution.py:154
  56.4 22.8 %collective-permute-start.7 = (bf16[384,384]{1,0:T(8,128)(2,1)}, bf16[384,384]{1,0:T(8,128)(2,1)}, u32[]{:S(2)}, u32[]{:S(2)}) collective-permute-start(bf16[384,384]{1,0:T(8,128)(2,1)} %maximum_select_fusion.5), channel_id=1, source_target_pairs={{0,8},{4,12},{8,16},{12,20},{16,24},{20,28},{24,32},{28,36},{32,40... | collective-permute-start | bytes 884744 | tf_op jit(solution)/shard_map/ppermute | solution.py:153
  61.5 19.6 %collective-permute-start.4 = (bf16[192,768]{1,0:T(8,128)(2,1)}, bf16[192,768]{1,0:T(8,128)(2,1)}, u32[]{:S(2)}, u32[]{:S(2)}) collective-permute-start(bf16[192,768]{1,0:T(8,128)(2,1)} %bitcast.72), channel_id=1, source_target_pairs={{0,0},{1,32},{2,64},{3,96},{32,1},{33,33},{34,65},{35,97},{64,2},{... | collective-permute-start | bytes 884744 | tf_op jit(solution)/shard_map/ppermute | solution.py:176
  68.5 12.5 %collective-permute-start.5 = (f32[768]{0:T(1024)S(1)}, f32[768]{0:T(1024)S(1)}, u32[]{:S(2)}, u32[]{:S(2)}) collective-permute-start(f32[768]{0:T(1024)S(1)} %reduce), channel_id=1, source_target_pairs={{0,0},{1,32},{2,64},{3,96},{32,1},{33,33},{34,65},{35,97},{64,2},{... | collective-permute-start | bytes 9224 | tf_op jit(solution)/shard_map/ppermute | solution.py:177
  83.4 1.0 copy-start.3
  84.9 7.6 %collective-permute-start.9 = (bf16[192,384]{0,1:T(8,128)(2,1)S(1)}, bf16[192,384]{0,1:T(8,128)(2,1)S(1)}, u32[]{:S(2)}, u32[]{:S(2)}) collective-permute-start(bf16[192,384]{0,1:T(8,128)(2,1)S(1)} %get-tuple-element.22), channel_id=1, source_target_pairs={{0,4},{4,0},{8,12},{12,8},{16,20},{20,16},{24,28},{28,24},{32,36},... | collective-permute-start | bytes 442376 | tf_op jit(solution)/shard_map/ppermute | solution.py:201
  93.8 17.0 %all-to-all-start.1 = ((bf16[4,192,768]{2,1,0:T(8,128)(2,1)}), bf16[4,192,768]{2,1,0:T(8,128)(2,1)S(1)}, u32[]{:S(2)}, u32[]{:S(2)}) async-start(bf16[4,192,768]{2,1,0:T(8,128)(2,1)} %broadcast_in_dim.31), calls=%async_computation.1 | async-start | bytes 2359296 | tf_op jit(solution)/shard_map/all_to_all | solution.py:208
  111.4 22.4 %collective-permute-start.12 = (bf16[192,768]{1,0:T(8,128)(2,1)S(1)}, bf16[192,768]{1,0:T(8,128)(2,1)S(1)}, u32[]{:S(2)}, u32[]{:S(2)}) collective-permute-start(bf16[192,768]{1,0:T(8,128)(2,1)S(1)} %convolution_convert_fusion), channel_id=1, source_target_pairs={{0,3},{1,0},{2,1},{3,2},{4,7},{5,4},{6,5},{7,6},{8,11},{9,8},{10,9... | collective-permute-start | bytes 884744 | tf_op jit(solution)/shard_map/ppermute | solution.py:219
  127.6 20.3 %collective-permute-start.11 = (bf16[192,768]{1,0:T(8,128)(2,1)}, bf16[192,768]{1,0:T(8,128)(2,1)S(1)}, u32[]{:S(2)}, u32[]{:S(2)}) collective-permute-start(bf16[192,768]{1,0:T(8,128)(2,1)} %convolution_convert_fusion.1), channel_id=1, source_target_pairs={{0,2},{1,3},{2,0},{3,1},{4,6},{5,7},{6,4},{7,5},{8,10},{9,11},{10,... | collective-permute-start | bytes 884744 | tf_op jit(solution)/shard_map/ppermute | solution.py:219
  130.8 17.1 %collective-permute-start.10 = (bf16[192,768]{1,0:T(8,128)(2,1)}, bf16[192,768]{1,0:T(8,128)(2,1)S(1)}, u32[]{:S(2)}, u32[]{:S(2)}) collective-permute-start(bf16[192,768]{1,0:T(8,128)(2,1)} %convolution_convert_fusion.2), channel_id=1, source_target_pairs={{0,1},{1,2},{2,3},{3,0},{4,5},{5,6},{6,7},{7,4},{8,9},{9,10},{10,1... | collective-permute-start | bytes 884744 | tf_op jit(solution)/shard_map/ppermute | solution.py:219
  149.5 22.9 %collective-permute-start.13 = (bf16[192,768]{1,0:T(8,128)(2,1)S(1)}, bf16[192,768]{1,0:T(8,128)(2,1)S(1)}, u32[]{:S(2)}, u32[]{:S(2)}) collective-permute-start(bf16[192,768]{1,0:T(8,128)(2,1)S(1)} %add_convert_fusion), channel_id=1, source_target_pairs={{0,128},{1,160},{2,192},{3,224},{32,129},{33,161},{34,193},{35,225... | collective-permute-start | bytes 884744 | tf_op jit(solution)/shard_map/ppermute | solution.py:227
